TPU v7x, 256 devices: a whole 4x4x8 slice. The times are simulated.
256 devices in a mesh: shards: 32 (over y, z), tensor: 2 (over core), sections: 4 (over x).
Axes of the slice: x: 4, y: 4, z: 8, core: 2. Of those that a mesh axis runs over, the one named last changes fastest.
Arguments:
- in_inputs: bfloat16 [4, 32, 1, 512, 768], P('sections', 'shards'), may hold values from -6 to 6
- in_cotangents: bfloat16 [4, 32, 1, 512, 1792], P('sections', 'shards', None, None, 'tensor'), may hold values from -1536 to 1536
- out_inputs: bfloat16 [4, 32, 1, 512, 1536], P('sections', 'shards', None, None, 'tensor'), may hold values from -6 to 6
- out_cotangents: bfloat16 [4, 32, 1, 512, 768], P('sections', 'shards'), may hold values from -1536 to 1536
- token_counts: int32 [32, 1], P('shards'), may hold values from 1 to 512, as said below
- in_error: float32 [4, 32, 768, 1792], P('sections', 'shards', None, 'tensor'), may hold values from -3 to 3
- out_error: float32 [4, 32, 1536, 768], P('sections', 'shards', 'tensor'), may hold values from -3 to 3
- in_query: float32 [4, 1792, 32], P('sections', 'tensor'), may hold values from -6 to 6
- out_query: float32 [4, 768, 32], P('sections'), may hold values from -6 to 6
- vec_grads: float32 [4, 32, 10568], P('sections', 'shards', 'tensor'), may hold values from -384 to 384
- in_weight: float32 [4, 768, 1792], P('sections', 'shards', 'tensor'), may hold values from -3 to 3
- in_moment: float32 [4, 768, 1792], P('sections', 'shards', 'tensor'), may hold values from -3 to 3
- out_weight: float32 [4, 1536, 768], P('sections', 'tensor', 'shards'), may hold values from -3 to 3
- out_moment: float32 [4, 1536, 768], P('sections', 'tensor', 'shards'), may hold values from -3 to 3
- vec_weight: float32 [4, 10568], P('sections', 'tensor'), may hold values from -3 to 3
- vec_moment: float32 [4, 10568], P('sections', 'tensor'), may hold values from -3 to 3
Outputs:
- new_in_error: float32 [4, 32, 768, 1792], P('sections', 'shards', None, 'tensor')
- new_out_error: float32 [4, 32, 1536, 768], P('sections', 'shards', 'tensor')
- new_in_weight: float32 [4, 768, 1792], P('sections', 'shards', 'tensor')
- new_in_moment: float32 [4, 768, 1792], P('sections', 'shards', 'tensor')
- new_out_weight: float32 [4, 1536, 768], P('sections', 'tensor', 'shards')
- new_out_moment: float32 [4, 1536, 768], P('sections', 'tensor', 'shards')
- new_vec_weight: float32 [4, 10568], P('sections', 'tensor')
- new_vec_moment: float32 [4, 10568], P('sections', 'tensor')
Inputs may be any that keep to these rules, and one draw needn't show every extreme that they name: `token_counts`: each count is between 1 and 512; some micro-batch is full.
All inputs are finite; a program needn't handle non-finite values.
Results may differ from a plain program's by a relative error of at most 0.0003.
Values sent between devices are 32-bit elements; how exact they have to be, the bound alone decides.
No kernel may reach another device: no remote copies, remote signals or barrier semaphores. Data moves between devices by JAX's collectives and lax.ppermute only.
A program may use at most 64 MiB of HBM per device.

v0:
```python
import jax
import jax.numpy as jnp
from jax import lax
from jax.sharding import PartitionSpec as P


def triangular_apply(left, gram):
    factor = jnp.linalg.cholesky(gram)
    return jax.scipy.linalg.solve_triangular(factor, left.T, lower=True).T


def gradient(inputs, cotangents, valid):
    width_a = inputs.shape[-1]
    width_b = cotangents.shape[-1]
    masked = cotangents[0, 0] * valid[..., None]
    return lax.dot_general(
        inputs[0, 0].reshape(-1, width_a),
        masked.reshape(-1, width_b),
        (((0,), (0,)), ((), ())),
        preferred_element_type=jnp.float32,
    )


def local(
    in_inputs,
    in_cotangents,
    out_inputs,
    out_cotangents,
    token_counts,
    in_error,
    out_error,
    in_query,
    out_query,
    vec_grads,
    in_weight,
    in_moment,
    out_weight,
    out_moment,
    vec_weight,
    vec_moment,
):
    highest = lax.Precision.HIGHEST
    contract = (((0,), (0,)), ((), ()))
    replicas = lax.axis_size("shards")
    shard_index = lax.axis_index("shards")
    position = jnp.arange(in_inputs.shape[3], dtype=jnp.int32)
    valid = (position[None, :] < token_counts[0][:, None]).astype(jnp.bfloat16)
    total = lax.psum(jnp.sum(token_counts).astype(jnp.float32), "shards")
    work_in = gradient(in_inputs, in_cotangents, valid) / total + in_error[0, 0]
    work_out = gradient(out_inputs, out_cotangents, valid) / total + out_error[0, 0]
    part_in = jnp.dot(work_in, in_query[0], precision=highest)
    part_out = jnp.dot(work_out, out_query[0], precision=highest)
    vec_part = vec_grads[0, 0]
    left_in = lax.psum(part_in, ("shards", "tensor"))
    left_out, vec_total = lax.psum((part_out, vec_part), "shards")
    ortho_in = triangular_apply(left_in, jnp.dot(left_in.T, left_in, precision=highest))
    gram_part = jnp.dot(left_out.T, left_out, precision=highest)
    ortho_out = triangular_apply(left_out, lax.psum(gram_part, "tensor"))
    right_part_in = lax.dot_general(work_in, ortho_in, contract, precision=highest)
    right_part_out = lax.dot_general(work_out, ortho_out, contract, precision=highest)
    right_in = lax.psum(right_part_in, "shards")
    right_out = lax.psum(right_part_out, ("shards", "tensor"))
    right_in = right_in / replicas
    right_out = right_out / replicas
    approx_in = jnp.dot(ortho_in, right_in.T, precision=highest)
    approx_out = jnp.dot(ortho_out, right_out.T, precision=highest)
    new_in_error = (work_in - approx_in)[None, None]
    new_out_error = (work_out - approx_out)[None, None]
    vec_mean = vec_total / total
    local_square = (
        jnp.sum(right_in * right_in)
        + 0.5 * jnp.sum(right_out * right_out)
        + jnp.sum(vec_mean * vec_mean)
    )
    square_sum = lax.psum(local_square, ("tensor", "sections"))
    factor = 1024.0 / jnp.sqrt(square_sum + 1e-06)
    row_count = in_weight.shape[1]
    shard_in = lax.dynamic_slice_in_dim(approx_in, shard_index * row_count, row_count, 0)
    col_count = out_weight.shape[2]
    shard_out = lax.dynamic_slice_in_dim(approx_out, shard_index * col_count, col_count, 1)
    new_in_moment = 0.9 * in_moment + factor * shard_in[None]
    new_out_moment = 0.9 * out_moment + factor * shard_out[None]
    new_vec_moment = 0.9 * vec_moment + factor * vec_mean[None]
    return (
        new_in_error,
        new_out_error,
        in_weight - 0.1 * new_in_moment,
        new_in_moment,
        out_weight - 0.1 * new_out_moment,
        new_out_moment,
        vec_weight - 0.1 * new_vec_moment,
        new_vec_moment,
    )


def solution(mesh):
    return jax.shard_map(
        local,
        mesh=mesh,
        in_specs=(
            P("sections", "shards", None, None, None),
            P("sections", "shards", None, None, "tensor"),
            P("sections", "shards", None, None, "tensor"),
            P("sections", "shards", None, None, None),
            P("shards", None),
            P("sections", "shards", None, "tensor"),
            P("sections", "shards", "tensor", None),
            P("sections", "tensor", None),
            P("sections", None, None),
            P("sections", "shards", "tensor"),
            P("sections", "shards", "tensor"),
            P("sections", "shards", "tensor"),
            P("sections", "tensor", "shards"),
            P("sections", "tensor", "shards"),
            P("sections", "tensor"),
            P("sections", "tensor"),
        ),
        out_specs=(
            P("sections", "shards", None, "tensor"),
            P("sections", "shards", "tensor", None),
            P("sections", "shards", "tensor"),
            P("sections", "shards", "tensor"),
            P("sections", "tensor", "shards"),
            P("sections", "tensor", "shards"),
            P("sections", "tensor"),
            P("sections", "tensor"),
        ),
        check_vma=False,
    )
```

profile of v0, /device:TPU:1, one launch (start us, length us, event | category | flops | bytes accessed | tf_op | source)
XLA Modules:
  0.0 715.9 jit_solution(11773875914962923723)
XLA Ops:
  8.7 3.0 copy.27
  11.8 118.9 %all-reduce.1 = (f32[]{:T(128)}, f32[5284]{0:T(1024)}) all-reduce(f32[]{:T(128)S(6)} %convert_element_type.13, f32[5284]{0:T(1024)S(1)} %reduce.4), channel_id=1, replica_groups=mesh['shards'=32,'tensor'=2,'sections'=4] {'shards'}, use_global_device_ids=true, to_apply=%region_0.0 | all-reduce | flops 5285 | bytes 42280 | tf_op jit(solution)/shard_map/psum | solution.py:48
  130.7 3.7 bitcast_add_fusion.1
  136.7 3.3 copy.24
  140.0 3.8 bitcast_add_fusion
  143.8 2.2 fusion.8
  146.0 151.1 %all-reduce.8.cloned.1.call-done = f32[768,32]{0,1:T(8,128)} async-done(((f32[768,32]{0,1:T(8,128)}), f32[768,32]{0,1:T(8,128)}) %all-reduce.8.cloned.1.call-update) | async-done | bytes 98320 | tf_op jit(solution)/shard_map/psum | solution.py:55
  299.0 8.8 %psum.60 = f32[32,32]{0,1:T(8,128)S(1)} all-reduce(f32[32,32]{0,1:T(8,128)} %fusion.33), channel_id=1, replica_groups=mesh['shards'=32,'tensor'=2,'sections'=4] {'tensor'}, use_global_device_ids=true, to_apply=%region_6.0 | all-reduce | flops 1024 | bytes 8192 | tf_op jit(solution)/shard_map/psum | solution.py:58
  309.8 3.6 cholesky.55
  315.4 3.2 custom-call.7
  320.4 4.5 fusion.34
  327.1 174.8 %all-reduce.10.cloned.1.call-done = (f32[768,32]{0,1:T(8,128)}, f32[768,32]{0,1:T(8,128)}) async-done(((f32[768,32]{0,1:T(8,128)}, f32[768,32]{0,1:T(8,128)}), (f32[768,32]{0,1:T(8,128)}, f32[768,32]{0,1:T(8,128)})) %all-reduce.10.cloned.1.call-update) | async-done | bytes 196624 | tf_op jit(solution)/shard_map/psum | solution.py:54
  501.9 4.4 fusion.18
  509.5 3.6 cholesky.44
  515.1 3.2 custom-call.6
  520.1 3.1 fusion.32
  523.2 4.1 subtract_bitcast_fusion.1
  528.6 132.9 %all-reduce.6.cloned.1.call-done = f32[896,32]{0,1:T(8,128)} async-done(((f32[896,32]{0,1:T(8,128)}), f32[896,32]{0,1:T(8,128)}) %all-reduce.6.cloned.1.call-update) | async-done | bytes 114704 | tf_op jit(solution)/shard_map/psum | solution.py:61
  664.3 3.0 copy.31
  667.4 20.2 %psum.63 = f32[]{:T(128)} all-reduce(f32[]{:T(128)S(6)} %add.56), channel_id=1, replica_groups=mesh['shards'=32,'tensor'=2,'sections'=4] {'tensor','sections'}, use_global_device_ids=true, to_apply=%region_12.15 | all-reduce | flops 1 | bytes 8 | tf_op jit(solution)/shard_map/psum | solution.py:75
  690.2 4.9 fusion.10
  695.1 3.3 copy.26
  698.4 3.7 subtract_bitcast_fusion
  702.1 3.4 copy.30
  (58 shorter events, 27.8 us)
Async XLA Ops:
  7.2 132.9 %copy-start = (bf16[1,1,1,512,768]{4,3,2,1,0:T(8,128)(2,1)S(1)}, bf16[1,1,1,512,768]{4,3,2,1,0:T(8,128)(2,1)}, u32[]{:S(2)}) copy-start(bf16[1,1,1,512,768]{4,3,2,1,0:T(8,128)(2,1)} %param.19) | copy-start | bytes 2359300
  7.2 290.0 %all-reduce.8.cloned.1.call-start = ((), (), s32[]{:S(2)}) async-start(), calls=%async_computation.1 | async-start | bytes 196608 | tf_op jit(solution)/shard_map/psum | solution.py:55
  130.7 3.7 copy-start.6
  134.5 2.3 copy-start.1
  136.7 365.2 %all-reduce.10.cloned.1.call-start = ((), (), s32[]{:S(2)}) async-start(), calls=%async_computation.2 | async-start | bytes 393216 | tf_op jit(solution)/shard_map/psum | solution.py:54
  140.0 3.8 copy-start.5
  319.7 0.6 copy-start.3
  324.9 336.6 %all-reduce.6.cloned.1.call-start = ((), (), s32[]{:S(2)}) async-start(), calls=%async_computation | async-start | bytes 229376 | tf_op jit(solution)/shard_map/psum | solution.py:61
  519.4 0.6 copy-start.2
  523.2 4.1 copy-start.4
  702.1 3.4 copy-start.10
  702.1 3.4 copy-start.11
  702.1 5.0 copy-start.8
  702.1 5.0 copy-start.9
  702.1 6.6 copy-start.7
  702.1 6.6 copy-start.12
  702.1 6.6 copy-start.13
Sparse Core Ops, SparseCore 0:
  136.8 160.3 all-reduce.7
  325.0 176.8 all-reduce.9
  523.3 138.1 all-reduce.5
where the time goes:
time: 717 us; the launch traced here: 716 us
  waiting for transfers between devices  459 us (64%)
  blocking collectives  148 us (21%)
  other arithmetic  38.6 us (5%)
  matrix products  34.2 us (5%)
  local copies, waits for them, and re-layouts  18.8 us (3%)
  between operations  17.3 us (2%)
    psum x1, waiting for transfers between devices, local(): left_in = lax.psum(part_in, ('shards', 'tensor'))  175 us
    psum x1, waiting for transfers between devices, local(): left_out, vec_total = lax.psum((part_out, vec_part), 'shards')  151 us
    psum x1, waiting for transfers between devices, local(): right_in = lax.psum(right_part_in, 'shards')  133 us
    psum x1, blocking collectives, local(): total = lax.psum(jnp.sum(token_counts).astype(jnp.float32), 'shards')  119 us
    psum x1, blocking collectives, local(): square_sum = lax.psum(local_square, ('tensor', 'sections'))  20.2 us
  transfers between devices with their start and end apart: 3, of which 3 were waited for; matrix products, arithmetic and copies ran while one was open for 2% of the time, Pallas kernels for 0%

commit v1 on v0

--- a/solution.py
+++ b/solution.py
@@ -58,7 +58,13 @@
     ortho_out = triangular_apply(left_out, lax.psum(gram_part, "tensor"))
     right_part_in = lax.dot_general(work_in, ortho_in, contract, precision=highest)
     right_part_out = lax.dot_general(work_out, ortho_out, contract, precision=highest)
-    right_in = lax.psum(right_part_in, "shards")
+    total_devices = jax.lax.axis_size("shards")
+    right_in = right_part_in
+    for hop_no in [rr for rr in (1, 2, 4, 8, 16) if rr < total_devices]:
+        x_next = jax.lax.ppermute(
+            right_in, "shards", [(j, j ^ hop_no) for j in range(total_devices)]
+        )
+        right_in = right_in + x_next
     right_out = lax.psum(right_part_out, ("shards", "tensor"))
     right_in = right_in / replicas
     right_out = right_out / replicas

time: 717 us -> 608 us (0.85)
  waiting for transfers between devices: 459 us -> 338 us
  starting transfers between devices: 0.3 us -> 12.1 us
    psum x1 -> x0, waiting for transfers between devices: 133 us -> none  [local(): right_in = lax.psum(right_part_in, 'shards')]
    ppermute x0 -> x5, starting transfers between devices: none -> 12 us  [local(): jax.lax.ppermute(right_in, 'shards', [(j, j ^ hop_no) for j in range(tota...]
    ppermute x0 -> x5, waiting for transfers between devices: none -> 9.38 us  [local(): jax.lax.ppermute(right_in, 'shards', [(j, j ^ hop_no) for j in range(tota...]
  transfers between devices with their start and end apart: 3 -> 7, of which waited for: 3 -> 6; matrix products, arithmetic and copies ran while one was open for 2% -> 3% of each run, Pallas kernels for 0% -> 0%
where the time goes in v1:
time: 608 us; the launch traced here: 607 us
  waiting for transfers between devices  338 us (56%)
  blocking collectives  149 us (25%)
  other arithmetic  38.2 us (6%)
  matrix products  32.9 us (5%)
  local copies, waits for them, and re-layouts  18.8 us (3%)
  between operations  17.6 us (3%)
  starting transfers between devices  12.1 us (2%)
    psum x1, waiting for transfers between devices, local(): left_in = lax.psum(part_in, ('shards', 'tensor'))  177 us
    psum x1, waiting for transfers between devices, local(): left_out, vec_total = lax.psum((part_out, vec_part), 'shards')  151 us
    psum x1, blocking collectives, local(): total = lax.psum(jnp.sum(token_counts).astype(jnp.float32), 'shards')  119 us
    psum x1, blocking collectives, local(): square_sum = lax.psum(local_square, ('tensor', 'sections'))  21.7 us
    unnamed x36, local copies, waits for them, and re-layouts  14.1 us
  transfers between devices with their start and end apart: 7, of which 6 were waited for; matrix products, arithmetic and copies ran while one was open for 3% of the time, Pallas kernels for 0%

profile of v1, /device:TPU:1, one launch (start us, length us, event | category | flops | bytes accessed | tf_op | source)
XLA Modules:
  0.0 607.1 jit_solution(5716441034992508917)
XLA Ops:
  8.7 3.0 copy.27
  11.8 118.9 %all-reduce.1 = (f32[]{:T(128)}, f32[5284]{0:T(1024)}) all-reduce(f32[]{:T(128)S(6)} %convert_element_type.13, f32[5284]{0:T(1024)S(1)} %reduce.4), channel_id=1, replica_groups=mesh['shards'=32,'tensor'=2,'sections'=4] {'shards'}, use_global_device_ids=true, to_apply=%region_0.0 | all-reduce | flops 5285 | bytes 42280 | tf_op jit(solution)/shard_map/psum | solution.py:48
  130.7 3.7 bitcast_add_fusion.1
  136.7 3.3 copy.24
  140.0 3.8 bitcast_add_fusion
  146.0 151.1 %all-reduce.5.cloned.1.call-done = f32[768,32]{0,1:T(8,128)} async-done(((f32[768,32]{0,1:T(8,128)}), f32[768,32]{0,1:T(8,128)}) %all-reduce.5.cloned.1.call-update) | async-done | bytes 98320 | tf_op jit(solution)/shard_map/psum | solution.py:55
  299.0 8.8 %psum.52 = f32[32,32]{0,1:T(8,128)S(1)} all-reduce(f32[32,32]{0,1:T(8,128)} %fusion.31), channel_id=1, replica_groups=mesh['shards'=32,'tensor'=2,'sections'=4] {'tensor'}, use_global_device_ids=true, to_apply=%region_5.0 | all-reduce | flops 1024 | bytes 8192 | tf_op jit(solution)/shard_map/psum | solution.py:58
  309.8 3.6 cholesky.55
  315.4 3.2 custom-call.7
  320.4 4.5 fusion.32
  324.9 177.5 %all-reduce.7.cloned.1.call-done = (f32[768,32]{0,1:T(8,128)}, f32[768,32]{0,1:T(8,128)}) async-done(((f32[768,32]{0,1:T(8,128)}, f32[768,32]{0,1:T(8,128)}), (f32[768,32]{0,1:T(8,128)}, f32[768,32]{0,1:T(8,128)})) %all-reduce.7.cloned.1.call-update) | async-done | bytes 196624 | tf_op jit(solution)/shard_map/psum | solution.py:54
  505.6 3.6 cholesky.44
  511.2 3.2 custom-call.6
  516.2 3.2 fusion.30
  524.2 4.6 collective-permute-start.1
  531.0 5.8 collective-permute-start.2
  536.9 3.0 fusion.16
  546.1 4.7 collective-permute-done.4
  553.7 3.0 copy.31
  556.7 21.7 %psum.55 = f32[]{:T(128)} all-reduce(f32[]{:T(128)S(6)} %add.74), channel_id=1, replica_groups=mesh['shards'=32,'tensor'=2,'sections'=4] {'tensor','sections'}, use_global_device_ids=true, to_apply=%region_11.14 | all-reduce | flops 1 | bytes 8 | tf_op jit(solution)/shard_map/psum | solution.py:81
  581.1 4.9 fusion.19
  586.0 3.3 copy.26
  589.3 3.7 subtract_bitcast_fusion
  593.0 3.4 copy.30
  (73 shorter events, 39.9 us)
Async XLA Ops:
  7.2 132.9 %copy-start = (bf16[1,1,1,512,768]{4,3,2,1,0:T(8,128)(2,1)S(1)}, bf16[1,1,1,512,768]{4,3,2,1,0:T(8,128)(2,1)}, u32[]{:S(2)}) copy-start(bf16[1,1,1,512,768]{4,3,2,1,0:T(8,128)(2,1)} %param.19) | copy-start | bytes 2359300
  7.2 290.0 %all-reduce.5.cloned.1.call-start = ((), (), s32[]{:S(2)}) async-start(), calls=%async_computation | async-start | bytes 196608 | tf_op jit(solution)/shard_map/psum | solution.py:55
  130.7 3.7 copy-start.8
  134.5 2.3 copy-start.1
  136.7 365.7 %all-reduce.7.cloned.1.call-start = ((), (), s32[]{:S(2)}) async-start(), calls=%async_computation.1 | async-start | bytes 393216 | tf_op jit(solution)/shard_map/psum | solution.py:54
  140.0 3.8 copy-start.7
  319.7 0.6 copy-start.5
  515.5 0.6 copy-start.4
  519.3 4.0 collective-permute-start
  520.7 19.4 %copy-start.2 = (f32[768,768]{0,1:T(8,128)S(1)}, f32[768,768]{0,1:T(8,128)}, u32[]{:S(2)}) copy-start(f32[768,768]{0,1:T(8,128)} %copy-done.1) | copy-start | bytes 7077892
  524.2 6.8 %collective-permute-start.1 = (f32[896,32]{0,1:T(8,128)S(1)}, f32[896,32]{0,1:T(8,128)S(1)}, u32[]{:S(2)}, u32[]{:S(2)}) collective-permute-start(f32[896,32]{0,1:T(8,128)S(1)} %add.67), channel_id=1, source_target_pairs={{0,16},{8,24},{16,0},{24,8},{32,48},{40,56},{48,32},{56,40},{64,80... | collective-permute-start | bytes 344072 | tf_op jit(solution)/shard_map/ppermute | solution.py:64
  531.0 8.9 %collective-permute-start.2 = (f32[896,32]{0,1:T(8,128)S(1)}, f32[896,32]{0,1:T(8,128)S(1)}, u32[]{:S(2)}, u32[]{:S(2)}) collective-permute-start(f32[896,32]{0,1:T(8,128)S(1)} %add.68), channel_id=1, source_target_pairs={{0,32},{8,40},{16,48},{24,56},{32,0},{40,8},{48,16},{56,24},{64,96... | collective-permute-start | bytes 344072 | tf_op jit(solution)/shard_map/ppermute | solution.py:64
  539.9 2.2 copy-start.3
  539.9 4.8 copy-start.6
  540.0 4.0 collective-permute-start.3
  544.7 6.1 %collective-permute-start.4 = (f32[896,32]{0,1:T(8,128)}, f32[896,32]{0,1:T(8,128)}, u32[]{:S(2)}, u32[]{:S(2)}) collective-permute-start(f32[896,32]{0,1:T(8,128)} %add.70), channel_id=1, source_target_pairs={{0,128},{8,136},{16,144},{24,152},{32,160},{40,168},{48,176},{56,1... | collective-permute-start | bytes 344072 | tf_op jit(solution)/shard_map/ppermute | solution.py:64
  593.0 3.4 copy-start.12
  593.0 3.4 copy-start.13
  593.0 5.0 copy-start.10
  593.0 5.0 copy-start.11
  593.0 6.6 %copy-start.9 = (f32[5284]{0:T(1024)S(1)}, f32[5284]{0:T(1024)}, u32[]{:S(2)}) copy-start(f32[5284]{0:T(1024)} %broadcast_multiply_fusion) | copy-start | bytes 63412
  593.0 6.6 %copy-start.14 = (f32[1,5284]{1,0:T(1,128)S(1)}, f32[1,5284]{1,0:T(1,128)}, u32[]{:S(2)}) copy-start(f32[1,5284]{1,0:T(1,128)} %param.33) | copy-start | bytes 63412
  593.0 6.6 %copy-start.15 = (f32[1,5284]{1,0:T(1,128)S(1)}, f32[1,5284]{1,0:T(1,128)}, u32[]{:S(2)}) copy-start(f32[1,5284]{1,0:T(1,128)} %param.34) | copy-start | bytes 63412
Sparse Core Ops, SparseCore 0:
  136.8 160.3 all-reduce.4
  325.0 177.2 all-reduce.6
